TPU v7x, 32 devices: a whole 2x2x4 slice. The times are simulated.
32 devices in a mesh: groups: 2 (over y), enc: 4 (over z), mp: 4 (over x, core).
Axes of the slice: x: 2, y: 2, z: 4, core: 2. Of those that a mesh axis runs over, the one named last changes fastest.
Arguments:
- hidden: bfloat16 [131072, 1024], P(('groups', 'enc'), 'mp'), parts along dimension 0, may hold values from -6 to 6
- proj_w: bfloat16 [1024, 128], P('mp'), may hold values from -0.1875 to 0.1875
- queries: bfloat16 [256, 32, 128], P(('groups', 'enc', 'mp')), parts along dimension 0, may hold values from -208 to 208
- lengths: int32 [512], P('groups'), parts along dimension 0, may hold values from 193 to 256, as said below
- candidates: int32 [256, 16], P(('groups', 'enc', 'mp')), parts along dimension 0, may hold values from 0 to 1023, as said below
Outputs:
- losses: float32 [256], P(('groups', 'enc', 'mp')), parts along dimension 0
- grad_w: float32 [2048, 128], P(('groups', 'mp')), parts along dimension 0
There are 2 independent parts, one for each index of `groups`. A program takes and returns all parts, laid end to end along the dimension named above; an argument that names none is the same for every part. Nothing has to cross between parts.
Inputs may be any that keep to these rules, and one draw needn't show every extreme that they name: Entries are global block numbers of this part. Of the candidates of the 8 queries of one device (aligned rows), at most 16 lie in the 64 blocks of any one device along enc+mp, where device k holds blocks k * 64 to (k + 1) * 64 - 1; some device receives exactly 16 from every device. Blocks may repeat. `lengths`: some passage has 256 tokens and some has 193.
All inputs are finite; a program needn't handle non-finite values.
Results may differ from a plain program's by a relative error of at most 0.0013.
The roundings to bfloat16 on the way count: a program that leaves them out, or rounds other values in their place, can miss the bound.
Values may be sent and summed in bfloat16 or wider, within the bound.
No kernel may reach another device: no remote copies, remote signals or barrier semaphores. Data moves between devices by JAX's collectives and lax.ppermute only.
A program may use at most 128 MiB of HBM per device.

v0:
```python
import jax
import jax.numpy as jnp
from jax import lax
from jax.sharding import PartitionSpec as P

L = 256
BLK = 64


def block_valid(block_ids, lengths):
    per_passage = L // BLK
    passage = block_ids // per_passage
    within = block_ids % per_passage
    positions = within[..., None] * BLK + jnp.arange(BLK, dtype=jnp.int32)
    return positions < lengths[passage][..., None]


def soft_max_sim(sim_tile, valid_mask):
    masked = jnp.where(valid_mask, sim_tile, jnp.float32(-1e30))
    peak = jnp.max(masked, -1, keepdims=True)
    shifted = jnp.exp(masked - peak)
    running = jnp.sum(shifted, -1, keepdims=True)
    scores = jnp.mean(peak[..., 0] + jnp.log(running[..., 0]), -1)
    weights = (shifted / running).astype(jnp.bfloat16)
    return (scores, weights)


def loss_terms(scores):
    margins = scores[:, 1:] - scores[:, :1]
    losses = jnp.mean(jax.nn.softplus(margins), 1)
    slopes = jax.nn.sigmoid(margins) / (scores.shape[1] - 1)
    d_score = jnp.concatenate([-jnp.sum(slopes, 1, keepdims=True), slopes], 1)
    return (losses, d_score)


def left_product(left, right):
    return lax.dot_general(
        left, right, (((0,), (0,)), ((), ())), preferred_element_type=jnp.float32
    )


def local(hidden, proj_w, queries, lengths, candidates):
    mp_count = lax.axis_size("mp")
    owners = lax.axis_size("enc") * mp_count
    row_share = hidden.shape[0] // mp_count
    emb_width = proj_w.shape[1]
    qry_dev = queries.shape[0]
    query_len = queries.shape[1]
    cand_count = candidates.shape[1]
    blk_dev = row_share // BLK
    slot_count = qry_dev * cand_count
    capacity = 2 * slot_count // owners
    e_pre = lax.psum_scatter(
        jnp.dot(hidden, proj_w, preferred_element_type=jnp.float32),
        "mp",
        scatter_dimension=0,
        tiled=True,
    )
    scale = lax.rsqrt(jnp.sum(e_pre * e_pre, -1, keepdims=True) + 1e-06)
    embedded = (e_pre * scale).astype(jnp.bfloat16)
    local_blocks = embedded.reshape(blk_dev, BLK, emb_width)
    flat_cand = candidates.reshape(-1)
    owner_of = flat_cand // blk_dev
    slot_ids = jnp.arange(slot_count, dtype=jnp.int32)
    same_owner = owner_of[:, None] == owner_of[None, :]
    earlier = slot_ids[None, :] < slot_ids[:, None]
    rank_in = jnp.sum(jnp.where(same_owner & earlier, 1, 0), 1).astype(jnp.int32)
    dest = owner_of * capacity + rank_in
    wanted = jnp.zeros((owners * capacity,), jnp.int32).at[dest].set(flat_cand % blk_dev)
    served = lax.all_to_all(
        wanted.reshape(owners, capacity), ("enc", "mp"), split_axis=0, concat_axis=0, tiled=True
    ).reshape(-1)
    grad_emb = jnp.zeros((blk_dev, BLK, emb_width), jnp.float32)
    tiles = local_blocks[served].reshape(owners, capacity, BLK, emb_width)
    arrived = lax.all_to_all(tiles, ("enc", "mp"), split_axis=0, concat_axis=0, tiled=True).reshape(
        owners * capacity, BLK, emb_width
    )
    mine = arrived[dest].reshape(qry_dev, cand_count, BLK, emb_width)
    valid_mask = block_valid(candidates, lengths)
    sim_tile = jnp.einsum("qie,qcje->qcij", queries, mine, preferred_element_type=jnp.float32)
    scores, weights = soft_max_sim(sim_tile, valid_mask[:, :, None, :])
    losses, d_score = loss_terms(scores)
    occ_grad = jnp.einsum("qcij,qie->qcje", weights, queries, preferred_element_type=jnp.float32)
    occ_grad = (occ_grad * (d_score / query_len)[:, :, None, None]).astype(jnp.bfloat16)
    outgoing = jnp.zeros((owners * capacity, BLK, emb_width), jnp.bfloat16)
    outgoing = outgoing.at[dest].set(occ_grad.reshape(slot_count, BLK, emb_width))
    returned = lax.all_to_all(
        outgoing.reshape(owners, capacity, BLK, emb_width),
        ("enc", "mp"),
        split_axis=0,
        concat_axis=0,
        tiled=True,
    )
    grad_emb = grad_emb.at[served].add(returned.reshape(-1, BLK, emb_width).astype(jnp.float32))
    grad_flat = grad_emb.reshape(row_share, emb_width)
    dot_e = jnp.sum(e_pre * grad_flat, -1, keepdims=True)
    de_pre = (scale * grad_flat - e_pre * (scale * scale * scale) * dot_e).astype(jnp.bfloat16)
    partial_w = left_product(hidden, lax.all_gather(de_pre, "mp", axis=0, tiled=True))
    grad_w = lax.psum(partial_w, "enc")
    return (losses, grad_w)


def solution(mesh):
    return jax.shard_map(
        local,
        mesh=mesh,
        in_specs=(
            P(("groups", "enc"), "mp"),
            P("mp", None),
            P(("groups", "enc", "mp"), None, None),
            P("groups"),
            P(("groups", "enc", "mp"), None),
        ),
        out_specs=(P(("groups", "enc", "mp")), P(("groups", "mp"), None)),
        check_vma=False,
    )
```

profile of v0, /device:TPU:0, one launch (start us, length us, event | category | flops | bytes accessed | tf_op | source)
XLA Modules:
  0.0 446.6 jit_solution(9475051947328319691)
XLA Ops:
  7.2 0.0 copy-start
  7.2 0.0 reduce-scatter.2.cloned.1.call-start
  7.2 0.8 copy-done
  8.0 8.9 %fusion.22 = f32[16384,128]{1,0:T(8,128)} fusion(bf16[16384,256]{1,0:T(8,128)(2,1)} %param.5, bf16[256,128]{1,0:T(8,128)(2,1)S(1)} %copy-done), kind=kOutput, calls=%fused_computation.74 | convolution fusion | flops 1073741824 | bytes 16842752 | tf_op jit(solution)/shard_map/dot_general | solution.py:54
  16.9 0.0 copy-start.6
  16.9 0.0 reduce-scatter.2.cloned.1.call-update
  17.0 0.7 copy-done.6
  17.6 0.1 reshape.243
  17.7 0.1 reshape.242
  17.8 0.2 select_reduce_fusion
  18.0 1.0 scatter_custom_fusion
  19.0 0.1 all_to_all.12
  19.1 13.6 %all_to_all.19 = s32[16,1,16]{2,1,0:T(1,128)S(1)} all-to-all(s32[16,1,16]{2,1,0:T(1,128)S(1)} %all_to_all.12), channel_id=1, replica_groups=mesh['groups'=2,'enc'=4,'mp'=4] {'enc','mp'}, dimensions={0} | all-to-all | bytes 2048 | tf_op jit(solution)/shard_map/all_to_all | solution.py:70
  32.7 0.5 broadcast.263
  33.2 0.7 reduce.5
  33.8 0.1 reshape.244
  33.9 57.6 %reduce-scatter.2.cloned.1.call-done = f32[4096,128]{1,0:T(8,128)} async-done(((f32[16384,128]{1,0:T(8,128)}), f32[4096,128]{1,0:T(8,128)}) %reduce-scatter.2.cloned.1.call-update) | async-done | bytes 2097168 | tf_op jit(solution)/shard_map/reduce_scatter | solution.py:53
  91.5 0.0 copy-start.2
  91.5 2.4 multiply_reduce_fusion
  93.9 0.0 copy-done.2
  93.9 0.7 multiply_convert_fusion.1
  94.6 3.1 gather_fusion.1
  97.7 4.8 %all-to-all-start.1 = ((bf16[16,16,64,128]{3,2,1,0:T(8,128)(2,1)}), bf16[16,16,64,128]{3,2,1,0:T(8,128)(2,1)}, u32[]{:S(2)}, u32[]{:S(2)}) async-start(bf16[16,16,64,128]{3,2,1,0:T(8,128)(2,1)} %bitcast.55), calls=%async_computation.2 | async-start | bytes 8388608 | tf_op jit(solution)/shard_map/all_to_all | solution.py:75
  102.5 0.0 copy-start.1
  102.5 0.0 all-gather.2.cloned.1.call-start
  102.6 0.1 reshape.254
  102.7 0.5 copy-done.1
  103.2 1.3 gather_fusion
  104.5 0.1 reshape.253
  104.5 0.1 add_compare_fusion
  104.7 75.5 %all-to-all-done.1 = bf16[16,16,64,128]{3,2,1,0:T(8,128)(2,1)} async-done(((bf16[16,16,64,128]{3,2,1,0:T(8,128)(2,1)}), bf16[16,16,64,128]{3,2,1,0:T(8,128)(2,1)}, u32[]{:S(2)}, u32[]{:S(2)}) %all-to-all-start.1) | async-done | bytes 4194336 | tf_op jit(solution)/shard_map/all_to_all | solution.py:75
  180.2 0.0 copy-start.5
  180.2 4.4 gather_fusion.2
  184.5 0.0 copy-done.5
  184.5 3.8 bitcast_reduce_fusion
  188.3 1.3 fusion.4
  189.6 0.1 add_reduce_fusion
  189.7 0.1 slice_reduce_fusion
  189.8 0.2 fusion.21
  190.1 0.1 copy.15
  190.2 0.1 maximum_multiply_fusion
  190.3 4.4 multiply_convert_fusion
  194.7 0.0 copy-start.4
  194.7 3.0 broadcast_in_dim.32
  197.7 0.0 copy-done.4
  197.7 15.7 %scatter_fusion = bf16[256,64,128]{2,1,0:T(8,128)(2,1)} fusion(bf16[256,64,128]{2,1,0:T(8,128)(2,1)} %broadcast_in_dim.32, s32[128]{0:T(128)S(1)} %fusion.17, bf16[128,64,128]{2,1,0:T(8,128)(2,1)S(1)} %bitcast.57), kind=kCustom, calls=%fused_computation.4 | custom fusion | bytes 6291968 | tf_op jit(solution)/shard_map/scatter | solution.py:86
  213.4 111.9 %all_to_all.20 = bf16[16,16,64,128]{3,2,1,0:T(8,128)(2,1)S(1)} all-to-all(bf16[16,16,64,128]{3,2,1,0:T(8,128)(2,1)} %bitcast.53), channel_id=1, replica_groups=mesh['groups'=2,'enc'=4,'mp'=4] {'enc','mp'}, dimensions={0} | all-to-all | bytes 8388608 | tf_op jit(solution)/shard_map/all_to_all | solution.py:87
  325.3 4.5 %bitcast_convert_fusion = f32[256,64,128]{2,1,0:T(8,128)} fusion(bf16[16,16,64,128]{3,2,1,0:T(8,128)(2,1)S(1)} %all_to_all.20), kind=kLoop, calls=%fused_computation.6 | loop fusion | flops 2097152 | bytes 12582912 | tf_op jit(solution)/shard_map/convert_element_type | solution.py:94
  329.8 0.2 broadcast_in_dim.31
  330.1 26.3 %scatter_fusion.1 = f32[64,64,128]{2,1,0:T(8,128)S(1)} fusion(f32[64,64,128]{2,1,0:T(8,128)S(1)} %broadcast_in_dim.31, s32[256]{0:T(256)S(1)} %bitcast.59, f32[256,64,128]{2,1,0:T(8,128)} %bitcast_convert_fusion), kind=kCustom, calls=%fused_computation.5 | custom fusion | flops 2097152 | bytes 25166848 | tf_op jit(solution)/shard_map/scatter-add | solution.py:94
  356.3 0.0 copy-start.3
  356.3 2.4 fusion.2
  358.7 0.0 copy-done.3
  358.7 3.0 fusion.1
  361.7 0.0 all-gather.2.cloned.1.call-update
  361.7 0.0 all-reduce.2.cloned.1.call-start
  361.8 35.2 %all-gather.2.cloned.1.call-done = bf16[16384,128]{1,0:T(8,128)(2,1)} async-done(((bf16[4096,128]{1,0:T(8,128)(2,1)}), bf16[16384,128]{1,0:T(8,128)(2,1)}) %all-gather.2.cloned.1.call-update) | async-done | bytes 4194320 | tf_op jit(solution)/shard_map/all_gather | solution.py:98
  397.0 6.8 %convolution_bitcast_fusion = f32[256,128]{0,1:T(8,128)} fusion(bf16[16384,128]{1,0:T(8,128)(2,1)} %all-gather.2.cloned.1.call-done, bf16[16384,256]{1,0:T(8,128)(2,1)} %param.5), kind=kOutput, calls=%fused_computation.20 | convolution fusion | flops 1073741824 | bytes 12713984 | tf_op jit(solution)/shard_map/dot_general | solution.py:37
  403.8 0.0 all-reduce.2.cloned.1.call-update
  403.8 0.5 broadcast_multiply_fusion.1
  404.3 34.1 %all-reduce.2.cloned.1.call-done = f32[256,128]{0,1:T(8,128)} async-done(((f32[256,128]{0,1:T(8,128)}), f32[256,128]{0,1:T(8,128)}) %all-reduce.2.cloned.1.call-update) | async-done | bytes 131088 | tf_op jit(solution)/shard_map/psum | solution.py:99
  438.4 1.7 copy.16
  (10 shorter events, 0.1 us)
Async XLA Ops:
  7.2 0.8 copy-start
  7.2 84.4 %reduce-scatter.2.cloned.1.call-start = ((), (), s32[]{:S(2)}) async-start(), calls=%async_computation.4 | async-start | bytes 10485760 | tf_op jit(solution)/shard_map/reduce_scatter | solution.py:53
  16.9 0.7 copy-start.6
  91.5 2.4 copy-start.2
  97.7 82.5 %all-to-all-start.1 = ((bf16[16,16,64,128]{3,2,1,0:T(8,128)(2,1)}), bf16[16,16,64,128]{3,2,1,0:T(8,128)(2,1)}, u32[]{:S(2)}, u32[]{:S(2)}) async-start(bf16[16,16,64,128]{3,2,1,0:T(8,128)(2,1)} %bitcast.55), calls=%async_computation.2 | async-start | bytes 8388608 | tf_op jit(solution)/shard_map/all_to_all | solution.py:75
  102.5 0.7 copy-start.1
  102.5 294.4 %all-gather.2.cloned.1.call-start = ((), (), s32[]{:S(2)}) async-start(), calls=%async_computation.5 | async-start | bytes 5242880 | tf_op jit(solution)/shard_map/all_gather | solution.py:98
  180.2 4.4 copy-start.5
  194.7 3.0 copy-start.4
  356.3 2.4 copy-start.3
  361.7 76.7 %all-reduce.2.cloned.1.call-start = ((), (), s32[]{:S(2)}) async-start(), calls=%async_computation.6 | async-start | bytes 262144 | tf_op jit(solution)/shard_map/psum | solution.py:99
Sparse Core Ops, SparseCore 0:
  17.1 74.3 reduce-scatter.1
  361.8 35.0 all-gather.1
  403.9 34.4 all-reduce.1
where the time goes:
time: 448 us; the launch traced here: 447 us
  waiting for transfers between devices  202 us (45%)
  blocking collectives  125 us (28%)
  other arithmetic  42.4 us (9%)
  local copies, waits for them, and re-layouts  33.4 us (7%)
  matrix products  24 us (5%)
  between operations  14 us (3%)
  starting transfers between devices  4.9 us (1%)
    all_to_all x1, blocking collectives, local(): lax.all_to_all(outgoing.reshape(owners, capacity, BLK, emb_width), ('enc'...  112 us
    all_to_all x1, waiting for transfers between devices, local(): lax.all_to_all(tiles, ('enc', 'mp'), split_axis=0, concat_axis=0, tiled=T...  75.5 us
    reduce_scatter x1, waiting for transfers between devices, local(): lax.psum_scatter(jnp.dot(hidden, proj_w, preferred_element_type=jnp.float...  57.6 us
    all_gather x1, waiting for transfers between devices, local(): lax.all_gather(de_pre, 'mp', axis=0, tiled=True)  35.2 us
    psum x1, waiting for transfers between devices, local(): grad_w = lax.psum(partial_w, 'enc')  34.1 us
    scatter-add x1, other arithmetic, local(): grad_emb.at[served]  26.3 us
    scatter x1, local copies, waits for them, and re-layouts, local(): outgoing.at[dest].set(occ_grad.reshape(slot_count, BLK, emb_width))  15.7 us
    all_to_all x1, blocking collectives, local(): lax.all_to_all(wanted.reshape(owners, capacity), ('enc', 'mp'), split_axi...  13.6 us
  transfers between devices with their start and end apart: 4, of which 4 were waited for; matrix products, arithmetic and copies ran while one was open for 1% of the time, Pallas kernels for 0%

commit v1 on v0

--- a/solution.py
+++ b/solution.py
@@ -5,6 +5,19 @@
 
 L = 256
 BLK = 64
+
+
+def collect(value, axis, dim):
+    size, index, span = (lax.axis_size(axis), lax.axis_index(axis), value.shape[dim])
+    forward = [(i, (i + 1) % size) for i in range(size)]
+    out = jnp.zeros((*value.shape[:dim], size * span, *value.shape[dim + 1 :]), value.dtype)
+    carried = value
+    for step in range(size):
+        owner = (index - step) % size
+        out = lax.dynamic_update_slice_in_dim(out, carried, owner * span, axis=dim)
+        if step < size - 1:
+            carried = lax.ppermute(carried, axis, forward)
+    return out
 
 
 def block_valid(block_ids, lengths):
@@ -95,7 +108,7 @@
     grad_flat = grad_emb.reshape(row_share, emb_width)
     dot_e = jnp.sum(e_pre * grad_flat, -1, keepdims=True)
     de_pre = (scale * grad_flat - e_pre * (scale * scale * scale) * dot_e).astype(jnp.bfloat16)
-    partial_w = left_product(hidden, lax.all_gather(de_pre, "mp", axis=0, tiled=True))
+    partial_w = left_product(hidden, collect(de_pre, "mp", 0))
     grad_w = lax.psum(partial_w, "enc")
     return (losses, grad_w)
 

time: 448 us -> 463 us (1.033)
  blocking collectives: 125 us -> 13.6 us
  waiting for transfers between devices: 202 us -> 299 us
  starting transfers between devices: 4.9 us -> 25.5 us
  local copies, waits for them, and re-layouts: 33.4 us -> 40.2 us
    all_to_all x1 -> x0, blocking collectives: 112 us -> none  [local(): lax.all_to_all(outgoing.reshape(owners, capacity, BLK, emb_width), ('enc'...]
    all_to_all x0 -> x1, waiting for transfers between devices: none -> 77.4 us  [local(): lax.all_to_all(outgoing.reshape(owners, capacity, BLK, emb_width), ('enc'...]
    ppermute x0 -> x3, waiting for transfers between devices: none -> 44.6 us  [collect(): carried = lax.ppermute(carried, axis, forward)]
    all_gather x1 -> x0, waiting for transfers between devices: 35.2 us -> none  [local(): lax.all_gather(de_pre, 'mp', axis=0, tiled=True)]
    all_to_all x0 -> x1, starting transfers between devices: none -> 19.7 us  [local(): lax.all_to_all(outgoing.reshape(owners, capacity, BLK, emb_width), ('enc'...]
    psum x1, waiting for transfers between devices: 34.1 us -> 44.1 us  [local(): grad_w = lax.psum(partial_w, 'enc')]
  transfers between devices with their start and end apart: 4 -> 7, of which waited for: 4 -> 7; matrix products, arithmetic and copies ran while one was open for 1% -> 1% of each run, Pallas kernels for 0% -> 0%
where the time goes in v1:
time: 463 us; the launch traced here: 461 us
  waiting for transfers between devices  299 us (65%)
  other arithmetic  43.9 us (9%)
  local copies, waits for them, and re-layouts  40.2 us (9%)
  starting transfers between devices  25.5 us (6%)
  matrix products  24 us (5%)
  between operations  14.3 us (3%)
  blocking collectives  13.6 us (3%)
    all_to_all x1, waiting for transfers between devices, local(): lax.all_to_all(outgoing.reshape(owners, capacity, BLK, emb_width), ('enc'...  77.4 us
    all_to_all x1, waiting for transfers between devices, local(): lax.all_to_all(tiles, ('enc', 'mp'), split_axis=0, concat_axis=0, tiled=T...  75.5 us
    reduce_scatter x1, waiting for transfers between devices, local(): lax.psum_scatter(jnp.dot(hidden, proj_w, preferred_element_type=jnp.float...  57.6 us
    ppermute x3, waiting for transfers between devices, collect(): carried = lax.ppermute(carried, axis, forward)  44.6 us
    psum x1, waiting for transfers between devices, local(): grad_w = lax.psum(partial_w, 'enc')  44.1 us
    scatter-add x1, other arithmetic, local(): grad_emb.at[served]  26.3 us
    all_to_all x1, starting transfers between devices, local(): lax.all_to_all(outgoing.reshape(owners, capacity, BLK, emb_width), ('enc'...  19.7 us
    scatter x1, local copies, waits for them, and re-layouts, local(): outgoing.at[dest].set(occ_grad.reshape(slot_count, BLK, emb_width))  15.7 us
  transfers between devices with their start and end apart: 7, of which 7 were waited for; matrix products, arithmetic and copies ran while one was open for 1% of the time, Pallas kernels for 0%

profile of v1, /device:TPU:0, one launch (start us, length us, event | category | flops | bytes accessed | tf_op | source)
XLA Modules:
  0.0 460.7 jit_solution(7581959835115146656)
XLA Ops:
  7.2 0.0 copy-start
  7.2 0.0 reduce-scatter.2.cloned.1.call-start
  7.2 0.8 copy-done
  8.0 8.9 %fusion.22 = f32[16384,128]{1,0:T(8,128)} fusion(bf16[16384,256]{1,0:T(8,128)(2,1)} %param.5, bf16[256,128]{1,0:T(8,128)(2,1)S(1)} %copy-done), kind=kOutput, calls=%fused_computation.78 | convolution fusion | flops 1073741824 | bytes 16842752 | tf_op jit(solution)/shard_map/dot_general | solution.py:67
  16.9 0.0 reduce-scatter.2.cloned.1.call-update
  17.0 0.7 copy-done.7
  17.6 0.1 reshape.243
  17.7 0.1 reshape.242
  17.8 0.2 select_reduce_fusion
  18.0 1.0 scatter_custom_fusion
  19.0 0.1 all_to_all.12
  19.1 13.6 %all_to_all.19 = s32[16,1,16]{2,1,0:T(1,128)S(1)} all-to-all(s32[16,1,16]{2,1,0:T(1,128)S(1)} %all_to_all.12), channel_id=1, replica_groups=mesh['groups'=2,'enc'=4,'mp'=4] {'enc','mp'}, dimensions={0} | all-to-all | bytes 2048 | tf_op jit(solution)/shard_map/all_to_all | solution.py:83
  32.7 0.5 broadcast.267
  33.2 0.7 reduce.5
  33.8 0.1 reshape.244
  33.9 57.6 %reduce-scatter.2.cloned.1.call-done = f32[4096,128]{1,0:T(8,128)} async-done(((f32[16384,128]{1,0:T(8,128)}), f32[4096,128]{1,0:T(8,128)}) %reduce-scatter.2.cloned.1.call-update) | async-done | bytes 2097168 | tf_op jit(solution)/shard_map/reduce_scatter | solution.py:66
  91.5 2.4 multiply_reduce_fusion
  93.9 0.0 copy-done.2
  93.9 0.7 multiply_convert_fusion.1
  94.6 3.1 gather_fusion.1
  97.7 4.8 %all-to-all-start.1 = ((bf16[16,16,64,128]{3,2,1,0:T(8,128)(2,1)}), bf16[16,16,64,128]{3,2,1,0:T(8,128)(2,1)}, u32[]{:S(2)}, u32[]{:S(2)}) async-start(bf16[16,16,64,128]{3,2,1,0:T(8,128)(2,1)} %bitcast.55), calls=%async_computation.2 | async-start | bytes 8388608 | tf_op jit(solution)/shard_map/all_to_all | solution.py:88
  102.5 0.0 copy-start.1
  102.5 0.1 reshape.254
  102.6 0.6 copy-done.1
  103.2 1.3 gather_fusion
  104.5 0.1 reshape.253
  104.5 0.1 add_compare_fusion
  104.7 75.5 %all-to-all-done.1 = bf16[16,16,64,128]{3,2,1,0:T(8,128)(2,1)} async-done(((bf16[16,16,64,128]{3,2,1,0:T(8,128)(2,1)}), bf16[16,16,64,128]{3,2,1,0:T(8,128)(2,1)}, u32[]{:S(2)}, u32[]{:S(2)}) %all-to-all-start.1) | async-done | bytes 4194336 | tf_op jit(solution)/shard_map/all_to_all | solution.py:88
  180.2 4.4 gather_fusion.2
  184.5 3.8 bitcast_reduce_fusion
  188.3 1.3 fusion.4
  189.6 0.1 add_reduce_fusion
  189.7 0.1 slice_reduce_fusion
  189.8 0.2 fusion.21
  190.1 0.1 copy.15
  190.2 0.1 maximum_multiply_fusion
  190.3 4.4 multiply_convert_fusion
  194.7 3.0 broadcast_in_dim.58
  197.7 15.7 %scatter_fusion = bf16[256,64,128]{2,1,0:T(8,128)(2,1)} fusion(bf16[256,64,128]{2,1,0:T(8,128)(2,1)} %broadcast_in_dim.58, s32[128]{0:T(128)S(1)} %fusion.17, bf16[128,64,128]{2,1,0:T(8,128)(2,1)S(1)} %bitcast.57), kind=kCustom, calls=%fused_computation.4 | custom fusion | bytes 6291968 | tf_op jit(solution)/shard_map/scatter | solution.py:99
  213.4 19.7 %all-to-all-start.2 = ((bf16[16,16,64,128]{3,2,1,0:T(8,128)(2,1)}), bf16[16,16,64,128]{3,2,1,0:T(8,128)(2,1)}, u32[]{:S(2)}, u32[]{:S(2)}) async-start(bf16[16,16,64,128]{3,2,1,0:T(8,128)(2,1)} %bitcast.53), calls=%async_computation.3 | async-start | bytes 8388608 | tf_op jit(solution)/shard_map/all_to_all | solution.py:100
  233.1 0.2 all-reduce.2.cloned.1.call-start
  233.3 77.4 %all-to-all-done.2 = bf16[16,16,64,128]{3,2,1,0:T(8,128)(2,1)} async-done(((bf16[16,16,64,128]{3,2,1,0:T(8,128)(2,1)}), bf16[16,16,64,128]{3,2,1,0:T(8,128)(2,1)}, u32[]{:S(2)}, u32[]{:S(2)}) %all-to-all-start.2) | async-done | bytes 4194336 | tf_op jit(solution)/shard_map/all_to_all | solution.py:100
  310.8 6.5 %bitcast_convert_fusion = f32[256,64,128]{2,1,0:T(8,128)} fusion(bf16[16,16,64,128]{3,2,1,0:T(8,128)(2,1)} %all-to-all-done.2), kind=kLoop, calls=%fused_computation.6 | loop fusion | flops 2097152 | bytes 12582912 | tf_op jit(solution)/shard_map/convert_element_type | solution.py:107
  317.2 0.2 broadcast_in_dim.34
  317.5 26.3 %scatter_fusion.1 = f32[64,64,128]{2,1,0:T(8,128)S(1)} fusion(f32[64,64,128]{2,1,0:T(8,128)S(1)} %broadcast_in_dim.34, s32[256]{0:T(256)S(1)} %bitcast.59, f32[256,64,128]{2,1,0:T(8,128)} %bitcast_convert_fusion), kind=kCustom, calls=%fused_computation.5 | custom fusion | flops 2097152 | bytes 25166848 | tf_op jit(solution)/shard_map/scatter-add | solution.py:107
  343.7 2.2 fusion.2
  345.9 0.6 broadcast_in_dim.33
  346.5 1.0 copy-done.3
  347.5 2.6 constant_dynamic-update-slice_fusion.3
  350.2 1.9 copy-done.4
  352.1 0.8 collective-permute-start
  352.9 18.3 %collective-permute-done = bf16[4096,128]{1,0:T(8,128)(2,1)S(1)} collective-permute-done((bf16[4096,128]{1,0:T(8,128)(2,1)S(1)}, bf16[4096,128]{1,0:T(8,128)(2,1)S(1)}, u32[]{:S(2)}, u32[]{:S(2)}) %collective-permute-start) | collective-permute-done | bytes 1048608 | tf_op jit(solution)/shard_map/ppermute | solution.py:19
  371.1 0.0 collective-permute-start.1
  371.1 14.2 %collective-permute-done.1 = bf16[4096,128]{1,0:T(8,128)(2,1)S(1)} collective-permute-done((bf16[4096,128]{1,0:T(8,128)(2,1)S(1)}, bf16[4096,128]{1,0:T(8,128)(2,1)S(1)}, u32[]{:S(2)}, u32[]{:S(2)}) %collective-permute-start.1) | collective-permute-done | bytes 1048608 | tf_op jit(solution)/shard_map/ppermute | solution.py:19
  385.4 0.0 collective-permute-start.2
  385.4 1.0 constant_dynamic-update-slice_fusion.2
  386.4 1.1 constant_dynamic-update-slice_fusion.1
  387.5 12.1 %collective-permute-done.2 = bf16[4096,128]{1,0:T(8,128)(2,1)S(1)} collective-permute-done((bf16[4096,128]{1,0:T(8,128)(2,1)S(1)}, bf16[4096,128]{1,0:T(8,128)(2,1)S(1)}, u32[]{:S(2)}, u32[]{:S(2)}) %collective-permute-start.2) | collective-permute-done | bytes 1048608 | tf_op jit(solution)/shard_map/ppermute | solution.py:19
  399.6 1.1 constant_dynamic-update-slice_fusion
  400.7 6.8 %convolution_bitcast_fusion = f32[256,128]{0,1:T(8,128)} fusion(bf16[16384,128]{1,0:T(8,128)(2,1)} %constant_dynamic-update-slice_fusion, bf16[16384,256]{1,0:T(8,128)(2,1)} %param.5), kind=kOutput, calls=%fused_computation.20 | convolution fusion | flops 1073741824 | bytes 12713984 | tf_op jit(solution)/shard_map/dot_general | solution.py:50
  407.5 0.0 all-reduce.2.cloned.1.call-update
  407.5 0.5 broadcast_multiply_fusion.1
  408.1 44.1 %all-reduce.2.cloned.1.call-done = f32[256,128]{0,1:T(8,128)} async-done(((f32[256,128]{0,1:T(8,128)}), f32[256,128]{0,1:T(8,128)}) %all-reduce.2.cloned.1.call-update) | async-done | bytes 131088 | tf_op jit(solution)/shard_map/psum | solution.py:112
  452.2 1.7 copy.16
  (18 shorter events, 0.1 us)
Async XLA Ops:
  7.2 0.8 copy-start
  7.2 84.4 %reduce-scatter.2.cloned.1.call-start = ((), (), s32[]{:S(2)}) async-start(), calls=%async_computation.4 | async-start | bytes 10485760 | tf_op jit(solution)/shard_map/reduce_scatter | solution.py:66
  16.9 0.7 copy-start.7
  91.5 2.4 copy-start.2
  97.7 82.5 %all-to-all-start.1 = ((bf16[16,16,64,128]{3,2,1,0:T(8,128)(2,1)}), bf16[16,16,64,128]{3,2,1,0:T(8,128)(2,1)}, u32[]{:S(2)}, u32[]{:S(2)}) async-start(bf16[16,16,64,128]{3,2,1,0:T(8,128)(2,1)} %bitcast.55), calls=%async_computation.2 | async-start | bytes 8388608 | tf_op jit(solution)/shard_map/all_to_all | solution.py:88
  102.5 0.7 copy-start.1
  180.2 4.4 copy-start.6
  194.7 3.0 copy-start.5
  213.4 97.4 %all-to-all-start.2 = ((bf16[16,16,64,128]{3,2,1,0:T(8,128)(2,1)}), bf16[16,16,64,128]{3,2,1,0:T(8,128)(2,1)}, u32[]{:S(2)}, u32[]{:S(2)}) async-start(bf16[16,16,64,128]{3,2,1,0:T(8,128)(2,1)} %bitcast.53), calls=%async_computation.3 | async-start | bytes 8388608 | tf_op jit(solution)/shard_map/all_to_all | solution.py:100
  233.1 219.1 %all-reduce.2.cloned.1.call-start = ((), (), s32[]{:S(2)}) async-start(), calls=%async_computation.5 | async-start | bytes 262144 | tf_op jit(solution)/shard_map/psum | solution.py:112
  345.9 1.6 copy-start.3
  350.2 1.9 copy-start.4
  352.1 19.0 %collective-permute-start = (bf16[4096,128]{1,0:T(8,128)(2,1)S(1)}, bf16[4096,128]{1,0:T(8,128)(2,1)S(1)}, u32[]{:S(2)}, u32[]{:S(2)}) collective-permute-start(bf16[4096,128]{1,0:T(8,128)(2,1)S(1)} %get-tuple-element.24), channel_id=1, source_target_pairs={{0,1},{1,2},{2,3},{3,0},{4,5},{5,6},{6,7},{7,4},{8,9},{9,10},{10,1... | collective-permute-start | bytes 3145736 | tf_op jit(solution)/shard_map/ppermute | solution.py:19
  371.1 14.2 %collective-permute-start.1 = (bf16[4096,128]{1,0:T(8,128)(2,1)S(1)}, bf16[4096,128]{1,0:T(8,128)(2,1)S(1)}, u32[]{:S(2)}, u32[]{:S(2)}) collective-permute-start(bf16[4096,128]{1,0:T(8,128)(2,1)S(1)} %collective-permute-done), channel_id=1, source_target_pairs={{0,1},{1,2},{2,3},{3,0},{4,5},{5,6},{6,7},{7,4},{8,9},{9,10},{10,1... | collective-permute-start | bytes 3145736 | tf_op jit(solution)/shard_map/ppermute | solution.py:19
  385.4 14.2 %collective-permute-start.2 = (bf16[4096,128]{1,0:T(8,128)(2,1)S(1)}, bf16[4096,128]{1,0:T(8,128)(2,1)S(1)}, u32[]{:S(2)}, u32[]{:S(2)}) collective-permute-start(bf16[4096,128]{1,0:T(8,128)(2,1)S(1)} %collective-permute-done.1), channel_id=1, source_target_pairs={{0,1},{1,2},{2,3},{3,0},{4,5},{5,6},{6,7},{7,4},{8,9},{9,10},{10,1... | collective-permute-start | bytes 3145736 | tf_op jit(solution)/shard_map/ppermute | solution.py:19
Sparse Core Ops, SparseCore 0:
  17.1 74.3 reduce-scatter.1
  407.7 44.4 all-reduce.1
